TPU v7x, 256 devices: a whole 4x4x8 slice. The times are simulated.
256 devices in a mesh: tiles: 64 (over y, z, core), cols: 4 (over x).
Axes of the slice: x: 4, y: 4, z: 8, core: 2. Of those that a mesh axis runs over, the one named last changes fastest.
Arguments:
- cov_blocks: bfloat16 [1024, 8, 256, 256], P('tiles', None, 'cols'), may hold values from -1 to 5, as said below
- neighbours: int32 [1024, 8], P('tiles'), may hold values from 0 to 1023, as said below
- voxel_mask: int32 [1024, 256], P('tiles', 'cols'), may hold values 0 or 1
- start_block: bfloat16 [128, 1024, 256], P('cols', 'tiles'), may hold values from -6 to 6
- overdensity: float32 [1024, 256], P('tiles', 'cols'), may hold values from -12 to 12
Outputs:
- basis_next: bfloat16 [128, 1024, 256], P('cols', 'tiles')
- coeffs: float32 [3, 128], replicated
Inputs may be any that keep to these rules, and one draw needn't show every extreme that they name: Slot 0 names the tile itself. Every other entry names another tile at most 3 away, counting cyclically (tile 1024 - 1 is next to tile 0), and some entry is exactly 3 away. If neighbours[i, k] = j then neighbours[j, k] = i. cov_blocks[j, k] is the transpose of cov_blocks[i, k] where neighbours[i, k] = j; the blocks of slot 0 are symmetric.
All inputs are finite; a program needn't handle non-finite values. No bound on the sum of `voxel_mask` on one device may be relied on, other than what follows from the above.
Results may differ from a plain program's by a relative error of at most 0.01.
The roundings to bfloat16 on the way count: a program that leaves them out, or rounds other values in their place, can miss the bound.
Values may be sent and summed in bfloat16 or wider, within the bound.
No kernel may reach another device: no remote copies, remote signals or barrier semaphores. Data moves between devices by JAX's collectives and lax.ppermute only.
A program may use at most 64 MiB of HBM per device.

v0:
```python
import math
import jax
import jax.numpy as jnp
from jax import lax
from jax.sharding import PartitionSpec as P

REACH = 3


def with_halo(cells, sides, width):
    for axis, dim in sides:
        count = lax.axis_size(axis)
        head = lax.slice_in_dim(cells, 0, width, axis=dim)
        tail = lax.slice_in_dim(cells, cells.shape[dim] - width, cells.shape[dim], axis=dim)
        cells = jnp.concatenate(
            [
                lax.ppermute(tail, axis, [(i, (i + 1) % count) for i in range(count)]),
                cells,
                lax.ppermute(head, axis, [((i + 1) % count, i) for i in range(count)]),
            ],
            axis=dim,
        )
    return cells


def orthonormal(work):
    gram = lax.psum(jnp.dot(work, work.T, preferred_element_type=jnp.float32), ("tiles", "cols"))
    lower = jnp.linalg.cholesky(gram)
    identity = jnp.eye(work.shape[0], dtype=jnp.float32)
    inverse = jax.scipy.linalg.solve_triangular(lower, identity, lower=True).astype(jnp.bfloat16)
    return jnp.dot(inverse, work, preferred_element_type=jnp.float32)


def projection(basis_flat, density):
    return jnp.sum(basis_flat.astype(jnp.float32) * density[None, :], axis=1)


def settle(terms):
    return lax.psum(terms, ("tiles", "cols"))


def fold_slots(total, piece, cov_blocks, local_index):
    for slot in range(cov_blocks.shape[1]):
        picked = jnp.take(piece, local_index[:, slot], axis=1)
        blocks = cov_blocks[:, slot]
        total = total + jnp.einsum(
            "iuv,biv->biu", blocks, picked, preferred_element_type=jnp.float32
        )
    return total


def local(cov_blocks, neighbours, voxel_mask, start_block, overdensity):
    tiles_here = neighbours.shape[0]
    voxels_here = voxel_mask.shape[1]
    voxels_all = cov_blocks.shape[3]
    cycle_size = tiles_here * lax.axis_size("tiles")
    first_tile = lax.axis_index("tiles") * tiles_here
    local_index = jnp.mod(neighbours - first_tile + REACH, cycle_size)
    mask_values = voxel_mask.astype(jnp.float32)
    density = overdensity.reshape(-1)
    start_cube = lax.all_to_all(start_block, "cols", split_axis=2, concat_axis=0, tiled=True)
    count = start_cube.shape[0]
    start_flat = (
        (start_cube.astype(jnp.float32) * mask_values[None]).astype(jnp.bfloat16).reshape(count, -1)
    )
    basis_now = orthonormal(start_flat).astype(jnp.bfloat16)
    basis_old = None
    found = []
    pending = projection(basis_now, density)
    found.append(settle(pending))
    rotated = None
    for lanczos_round in range(2):
        image_count = basis_now.shape[0]
        basis_cube = basis_now.reshape(image_count, tiles_here, voxels_here)
        empty = jnp.zeros((image_count, tiles_here, voxels_here), jnp.float32)
        gathered = lax.all_gather(basis_cube, "cols", axis=2, tiled=True)
        padded = with_halo(gathered, (("tiles", 1),), REACH)
        total = fold_slots(empty, padded, cov_blocks, local_index)
        image = (total * mask_values[None]).astype(jnp.bfloat16).reshape(image_count, -1)
        if basis_old is None:
            stacked = basis_now
        else:
            stacked = jnp.concatenate([basis_now, basis_old], axis=0)
        local_sums = jnp.dot(stacked, image.T, preferred_element_type=jnp.float32)
        sums = lax.psum(local_sums, ("tiles", "cols"))
        along = sums[:count].astype(jnp.bfloat16)
        resid = image.astype(jnp.float32) - jnp.dot(
            along.T, basis_now, preferred_element_type=jnp.float32
        )
        if basis_old is not None:
            back = sums[count:].astype(jnp.bfloat16)
            resid = resid - jnp.dot(back.T, basis_old, preferred_element_type=jnp.float32)
        rotated = orthonormal(resid.astype(jnp.bfloat16))
        basis_old, basis_now = (basis_now, rotated.astype(jnp.bfloat16))
        pending = projection(basis_now, density)
        found.append(settle(pending))
    coeffs = jnp.stack(found)
    scaled = (rotated * math.sqrt(cycle_size * voxels_all)).astype(jnp.bfloat16)
    scaled = scaled.reshape(count, tiles_here, voxels_here)
    basis_next = lax.all_to_all(scaled, "cols", split_axis=0, concat_axis=2, tiled=True)
    return (basis_next, coeffs)


def solution(mesh):
    return jax.shard_map(
        local,
        mesh=mesh,
        in_specs=(
            P("tiles", None, "cols", None),
            P("tiles", None),
            P("tiles", "cols"),
            P("cols", "tiles", None),
            P("tiles", "cols"),
        ),
        out_specs=(P("cols", "tiles", None), P()),
        check_vma=False,
    )
```

profile of v0, /device:TPU:1, one launch (start us, length us, event | category | flops | bytes accessed | tf_op | source)
XLA Modules:
  0.0 1190.3 jit_solution(6091634544763093636)
XLA Ops:
  7.2 2.4 copy.138
  9.5 1.7 reshape.230
  11.2 4.8 all-to-all-start
  16.7 4.8 all-to-all-done
  24.7 244.0 %all-reduce.6.cloned.1.call-done = f32[128,128]{0,1:T(8,128)} async-done(((f32[128,128]{0,1:T(8,128)}), f32[128,128]{0,1:T(8,128)}) %all-reduce.6.cloned.1.call-update) | async-done | bytes 65552 | tf_op jit(solution)/shard_map/psum | solution.py:27
  270.5 11.7 cholesky.59
  283.5 9.8 custom-call.7
  295.1 20.7 %all-gather.3.cloned.1.call-done = bf16[128,16,256]{0,1,2:T(8,128)(2,1)} async-done(((bf16[128,16,64]{0,1,2:T(8,128)(2,1)}), bf16[128,16,256]{0,1,2:T(8,128)(2,1)}) %all-gather.3.cloned.1.call-update) | async-done | bytes 1048592 | tf_op jit(solution)/shard_map/all_gather | solution.py:76
  315.8 1.6 copy.147
  317.5 17.0 %collective-permute-start = (bf16[128,3,256]{2,0,1:T(8,128)(2,1)S(1)}, bf16[128,3,256]{2,0,1:T(8,128)(2,1)S(1)}, u32[]{:S(2)}, u32[]{:S(2)}) collective-permute-start(bf16[128,3,256]{2,0,1:T(8,128)(2,1)S(1)} %get-tuple-element.29), channel_id=1, source_target_pairs={{0,4},{4,8},{8,12},{12,16},{16,20},{20,24},{24,28},{28,32},{32,36}... | collective-permute-start | bytes 589832 | tf_op jit(solution)/shard_map/ppermute | solution.py:17
  334.5 2.6 collective-permute-done
  337.1 2.8 collective-permute-done.1
  340.0 1.6 gather_fusion.1
  341.6 1.6 gather_fusion
  343.3 1.6 gather_fusion.2
  344.9 1.6 gather_fusion.3
  346.4 1.6 gather_fusion.4
  348.0 1.6 gather_fusion.5
  349.6 1.6 gather_fusion.6
  351.9 2.1 fusion.21
  354.0 2.1 convolution_add_fusion.13
  356.1 1.7 convolution_add_fusion.12
  361.1 78.1 %psum.57 = bf16[128,128]{1,0:T(8,128)(2,1)S(1)} all-reduce(f32[128,128]{1,0:T(8,128)S(1)} %fusion.149), channel_id=1, replica_groups=mesh['tiles'=64,'cols'=4] {'tiles','cols'}, use_global_device_ids=true, to_apply=%region_3.7 | all-reduce | flops 16384 | bytes 98304 | tf_op jit(solution)/shard_map/psum | solution.py:85
  440.4 237.6 %all-reduce.8.cloned.1.call-done = f32[128,128]{0,1:T(8,128)} async-done(((f32[128,128]{0,1:T(8,128)}), f32[128,128]{0,1:T(8,128)}) %all-reduce.8.cloned.1.call-update) | async-done | bytes 65552 | tf_op jit(solution)/shard_map/psum | solution.py:27
  679.8 11.7 cholesky.70
  692.9 9.8 custom-call.8
  704.3 20.8 %all-gather.5.cloned.1.call-done = bf16[128,16,256]{0,1,2:T(8,128)(2,1)} async-done(((bf16[128,16,64]{0,1,2:T(8,128)(2,1)}), bf16[128,16,256]{0,1,2:T(8,128)(2,1)}) %all-gather.5.cloned.1.call-update) | async-done | bytes 1048592 | tf_op jit(solution)/shard_map/all_gather | solution.py:76
  725.1 1.6 copy.163
  726.8 4.0 collective-permute-start.2
  730.8 2.6 collective-permute-done.2
  733.4 2.8 collective-permute-done.3
  736.4 1.6 gather_fusion.9
  738.0 1.6 gather_fusion.8
  739.6 1.6 gather_fusion.10
  741.2 1.6 gather_fusion.11
  742.8 1.6 gather_fusion.12
  744.4 1.6 gather_fusion.13
  746.0 1.6 gather_fusion.14
  748.2 2.1 fusion.12
  750.3 2.1 convolution_add_fusion.6
  752.5 1.7 convolution_add_fusion.5
  757.5 78.5 %all-reduce.11 = bf16[256,128]{1,0:T(8,128)(2,1)S(1)} all-reduce(f32[256,128]{1,0:T(8,128)S(1)} %fusion.56), channel_id=1, replica_groups=mesh['tiles'=64,'cols'=4] {'tiles','cols'}, use_global_device_ids=true, to_apply=%region_5.9 | all-reduce | flops 32768 | bytes 196608 | tf_op jit(solution)/shard_map/psum | solution.py:85
  837.5 237.6 %all-reduce.10.cloned.1.call-done = f32[128,128]{0,1:T(8,128)} async-done(((f32[128,128]{0,1:T(8,128)}), f32[128,128]{0,1:T(8,128)}) %all-reduce.10.cloned.1.call-update) | async-done | bytes 65552 | tf_op jit(solution)/shard_map/psum | solution.py:27
  1076.9 11.7 cholesky.81
  1090.0 9.8 custom-call.9
  1101.0 1.1 reshape.232
  1102.1 3.4 all-to-all-start.1
  1105.5 75.5 %all-reduce = (f32[1,128]{1,0:T(1,128)S(1)}, f32[1,128]{1,0:T(1,128)S(1)}, f32[1,128]{1,0:T(1,128)S(1)}) all-reduce(f32[1,128]{1,0:T(1,128)S(1)} %bitcast.212, f32[1,128]{1,0:T(1,128)S(1)} %bitcast.211, f32[1,128]{1,0:T(1,128)S(1)} %bitcast.210), channel_id=1, replica_groups=mesh['tiles'=64,'cols'=4] {'tiles','cols'}, use_global_device_ids=true, to_apply=%region_12.16 | all-reduce | flops 384 | bytes 3072 | tf_op jit(solution)/shard_map/psum | solution.py:39
  (111 shorter events, 30.7 us)
Async XLA Ops:
  11.2 10.4 all-to-all-start
  16.0 252.7 %all-reduce.6.cloned.1.call-start = ((), (), s32[]{:S(2)}) async-start(), calls=%async_computation.2 | async-start | bytes 131072 | tf_op jit(solution)/shard_map/psum | solution.py:27
  22.1 272.9 %copy-start.11 = (s32[16,8]{0,1:T(8,128)S(1)}, s32[16,8]{0,1:T(8,128)}, u32[]{:S(2)}) copy-start(s32[16,8]{0,1:T(8,128)} %param.11) | copy-start | bytes 1540
  24.2 291.6 %all-gather.3.cloned.1.call-start = ((), (), s32[]{:S(2)}) async-start(), calls=%async_computation.3 | async-start | bytes 1310720 | tf_op jit(solution)/shard_map/all_gather | solution.py:76
  294.9 383.1 %all-reduce.8.cloned.1.call-start = ((), (), s32[]{:S(2)}) async-start(), calls=%async_computation.4 | async-start | bytes 131072 | tf_op jit(solution)/shard_map/psum | solution.py:27
  317.5 19.6 %collective-permute-start = (bf16[128,3,256]{2,0,1:T(8,128)(2,1)S(1)}, bf16[128,3,256]{2,0,1:T(8,128)(2,1)S(1)}, u32[]{:S(2)}, u32[]{:S(2)}) collective-permute-start(bf16[128,3,256]{2,0,1:T(8,128)(2,1)S(1)} %get-tuple-element.29), channel_id=1, source_target_pairs={{0,4},{4,8},{8,12},{12,16},{16,20},{20,24},{24,28},{28,32},{32,36}... | collective-permute-start | bytes 589832 | tf_op jit(solution)/shard_map/ppermute | solution.py:17
  334.5 5.4 collective-permute-start.1
  351.9 4.2 copy-start.9
  351.9 6.0 copy-start.8
  351.9 6.0 copy-start.12
  354.0 4.5 copy-start.7
  356.1 2.9 copy-start.6
  357.9 1.7 copy-start.4
  440.3 284.8 %all-gather.5.cloned.1.call-start = ((), (), s32[]{:S(2)}) async-start(), calls=%async_computation.5 | async-start | bytes 1310720 | tf_op jit(solution)/shard_map/all_gather | solution.py:76
  704.3 370.8 %all-reduce.10.cloned.1.call-start = ((), (), s32[]{:S(2)}) async-start(), calls=%async_computation.6 | async-start | bytes 131072 | tf_op jit(solution)/shard_map/psum | solution.py:27
  726.8 6.6 collective-permute-start.2
  730.8 5.4 collective-permute-start.3
  748.2 4.2 copy-start.5
  748.2 6.0 copy-start.3
  748.2 6.0 copy-start.13
  750.3 4.5 copy-start.2
  752.5 2.9 copy-start.1
  754.2 1.7 copy-start
  756.5 80.9 %copy-start.10 = (f32[16,64]{1,0:T(8,128)S(1)}, f32[16,64]{1,0:T(8,128)}, u32[]{:S(2)}) copy-start(f32[16,64]{1,0:T(8,128)} %param.14) | copy-start | bytes 12292
  1102.1 79.5 %all-to-all-start.1 = ((bf16[4,2,16384]{2,1,0:T(2,128)(2,1)}), bf16[4,2,16384]{2,1,0:T(2,128)(2,1)S(1)}, u32[]{:S(2)}, u32[]{:S(2)}) async-start(bf16[4,2,16384]{2,1,0:T(2,128)(2,1)} %reshape.232), calls=%async_computation.1 | async-start | bytes 524288 | tf_op jit(solution)/shard_map/all_to_all | solution.py:100
Sparse Core Ops, SparseCore 0:
  24.4 244.2 all-reduce.5
  295.1 20.7 all-gather.2
  440.5 237.5 all-reduce.7
  704.4 20.7 all-gather.4
  837.5 237.5 all-reduce.9
where the time goes:
time: 1200 us; the launch traced here: 1190 us
  waiting for transfers between devices  776 us (65%)
  blocking collectives  232 us (19%)
  other arithmetic  72.9 us (6%)
  local copies, waits for them, and re-layouts  41.8 us (3%)
  starting transfers between devices  29.4 us (2%)
  matrix products  23 us (2%)
  between operations  14.8 us (1%)
    psum x3, waiting for transfers between devices, orthonormal(): lax.psum(jnp.dot(work, work.T, preferred_element_type=jnp.float32), ('til...  719 us
    psum x2, blocking collectives, local(): sums = lax.psum(local_sums, ('tiles', 'cols'))  157 us
    psum x1, blocking collectives, settle(): return lax.psum(terms, ('tiles', 'cols'))  75.5 us
    all_gather x2, waiting for transfers between devices, local(): gathered = lax.all_gather(basis_cube, 'cols', axis=2, tiled=True)  41.6 us
    another operation x9, other arithmetic, orthonormal(): lower = jnp.linalg.cholesky(gram)  37.2 us
    another operation x6, other arithmetic, orthonormal(): jax.scipy.linalg.solve_triangular(lower, identity, lower=True)  31.4 us
  transfers between devices with their start and end apart: 11, of which 10 were waited for; matrix products, arithmetic and copies ran while one was open for 0% of the time, Pallas kernels for 0%

commit v1 on v0

--- a/solution.py
+++ b/solution.py
@@ -82,7 +82,7 @@
         else:
             stacked = jnp.concatenate([basis_now, basis_old], axis=0)
         local_sums = jnp.dot(stacked, image.T, preferred_element_type=jnp.float32)
-        sums = lax.psum(local_sums, ("tiles", "cols"))
+        sums = jnp.sum(lax.all_gather(local_sums, ("tiles", "cols")), axis=0)
         along = sums[:count].astype(jnp.bfloat16)
         resid = image.astype(jnp.float32) - jnp.dot(
             along.T, basis_now, preferred_element_type=jnp.float32

time: 1200 us -> 1340 us (1.12)
  waiting for transfers between devices: 776 us -> 1060 us
  blocking collectives: 232 us -> 75.5 us
  other arithmetic: 72.9 us -> 91.7 us
    all_gather x0 -> x2, waiting for transfers between devices: none -> 277 us  [local(): sums = jnp.sum(lax.all_gather(local_sums, ('tiles', 'cols')), axis=0)]
    psum x2 -> x0, blocking collectives: 157 us -> none  [local(): sums = lax.psum(local_sums, ('tiles', 'cols'))]
    reduce_sum x0 -> x2, other arithmetic: none -> 18.8 us  [local(): sums = jnp.sum(lax.all_gather(local_sums, ('tiles', 'cols')), axis=0)]
  transfers between devices with their start and end apart: 11 -> 13, of which waited for: 10 -> 12; matrix products, arithmetic and copies ran while one was open for 0% -> 0% of each run, Pallas kernels for 0% -> 0%
where the time goes in v1:
time: 1340 us; the launch traced here: 1330 us
  waiting for transfers between devices  1060 us (79%)
  other arithmetic  91.7 us (7%)
  blocking collectives  75.5 us (6%)
  local copies, waits for them, and re-layouts  41.8 us (3%)
  starting transfers between devices  29.6 us (2%)
  matrix products  24.2 us (2%)
  between operations  15.1 us (1%)
    psum x3, waiting for transfers between devices, orthonormal(): lax.psum(jnp.dot(work, work.T, preferred_element_type=jnp.float32), ('til...  721 us
    all_gather x2, waiting for transfers between devices, local(): sums = jnp.sum(lax.all_gather(local_sums, ('tiles', 'cols')), axis=0)  277 us
    psum x1, blocking collectives, settle(): return lax.psum(terms, ('tiles', 'cols'))  75.5 us
    all_gather x2, waiting for transfers between devices, local(): gathered = lax.all_gather(basis_cube, 'cols', axis=2, tiled=True)  41.6 us
    another operation x9, other arithmetic, orthonormal(): lower = jnp.linalg.cholesky(gram)  37.2 us
    another operation x6, other arithmetic, orthonormal(): jax.scipy.linalg.solve_triangular(lower, identity, lower=True)  31.4 us
  transfers between devices with their start and end apart: 13, of which 12 were waited for; matrix products, arithmetic and copies ran while one was open for 0% of the time, Pallas kernels for 0%

profile of v1, /device:TPU:1, one launch (start us, length us, event | category | flops | bytes accessed | tf_op | source)
XLA Modules:
  0.0 1333.8 jit_solution(14685793195251824897)
XLA Ops:
  7.2 2.4 copy.138
  9.5 1.7 reshape.232
  11.2 4.8 all-to-all-start
  16.7 4.8 all-to-all-done
  24.7 244.1 %all-reduce.5.cloned.1.call-done = f32[128,128]{0,1:T(8,128)} async-done(((f32[128,128]{0,1:T(8,128)}), f32[128,128]{0,1:T(8,128)}) %all-reduce.5.cloned.1.call-update) | async-done | bytes 65552 | tf_op jit(solution)/shard_map/psum | solution.py:27
  270.5 11.7 cholesky.59
  283.6 9.8 custom-call.7
  295.1 20.7 %all-gather.7.cloned.1.call-done = bf16[128,16,256]{0,1,2:T(8,128)(2,1)} async-done(((bf16[128,16,64]{0,1,2:T(8,128)(2,1)}), bf16[128,16,256]{0,1,2:T(8,128)(2,1)}) %all-gather.7.cloned.1.call-update) | async-done | bytes 1048592 | tf_op jit(solution)/shard_map/all_gather | solution.py:76
  315.9 1.6 copy.147
  317.5 16.9 %collective-permute-start = (bf16[128,3,256]{2,0,1:T(8,128)(2,1)S(1)}, bf16[128,3,256]{2,0,1:T(8,128)(2,1)S(1)}, u32[]{:S(2)}, u32[]{:S(2)}) collective-permute-start(bf16[128,3,256]{2,0,1:T(8,128)(2,1)S(1)} %get-tuple-element.29), channel_id=1, source_target_pairs={{0,4},{4,8},{8,12},{12,16},{16,20},{20,24},{24,28},{28,32},{32,36}... | collective-permute-start | bytes 589832 | tf_op jit(solution)/shard_map/ppermute | solution.py:17
  334.5 2.6 collective-permute-done
  337.1 2.8 collective-permute-done.1
  340.0 1.6 gather_fusion.1
  341.6 1.6 gather_fusion
  343.3 1.6 gather_fusion.2
  344.9 1.6 gather_fusion.3
  346.5 1.6 gather_fusion.4
  348.0 1.6 gather_fusion.5
  349.7 1.6 gather_fusion.6
  351.9 2.1 fusion.21
  354.0 2.1 convolution_add_fusion.13
  356.2 1.7 convolution_add_fusion.12
  361.8 125.4 %all-gather.11.cloned.1.call-done = f32[32768,128]{1,0:T(8,128)} async-done(((f32[128,128]{1,0:T(8,128)}), f32[32768,128]{1,0:T(8,128)}) %all-gather.11.cloned.1.call-update) | async-done | bytes 16777232 | tf_op jit(solution)/shard_map/all_gather | solution.py:85
  487.2 6.6 reduce_sum.45
  495.0 238.6 %all-reduce.7.cloned.1.call-done = f32[128,128]{0,1:T(8,128)} async-done(((f32[128,128]{0,1:T(8,128)}), f32[128,128]{0,1:T(8,128)}) %all-reduce.7.cloned.1.call-update) | async-done | bytes 65552 | tf_op jit(solution)/shard_map/psum | solution.py:27
  735.4 11.7 cholesky.70
  748.5 9.8 custom-call.8
  759.9 20.8 %all-gather.9.cloned.1.call-done = bf16[128,16,256]{0,1,2:T(8,128)(2,1)} async-done(((bf16[128,16,64]{0,1,2:T(8,128)(2,1)}), bf16[128,16,256]{0,1,2:T(8,128)(2,1)}) %all-gather.9.cloned.1.call-update) | async-done | bytes 1048592 | tf_op jit(solution)/shard_map/all_gather | solution.py:76
  780.8 1.6 copy.163
  782.4 4.0 collective-permute-start.2
  786.4 2.6 collective-permute-done.2
  789.0 2.8 collective-permute-done.3
  792.0 1.6 gather_fusion.9
  793.6 1.6 gather_fusion.8
  795.2 1.6 gather_fusion.10
  796.8 1.6 gather_fusion.11
  800.0 1.6 gather_fusion.13
  801.6 1.6 gather_fusion.14
  803.9 2.1 fusion.12
  805.9 2.1 convolution_add_fusion.6
  808.1 1.7 convolution_add_fusion.5
  814.0 152.1 %all-gather.13.cloned.1.call-done = f32[65536,128]{1,0:T(8,128)} async-done(((f32[256,128]{1,0:T(8,128)}), f32[65536,128]{1,0:T(8,128)}) %all-gather.13.cloned.1.call-update) | async-done | bytes 33554448 | tf_op jit(solution)/shard_map/all_gather | solution.py:85
  966.1 12.2 reduce_sum.46
  979.8 238.5 %all-reduce.9.cloned.1.call-done = f32[128,128]{0,1:T(8,128)} async-done(((f32[128,128]{0,1:T(8,128)}), f32[128,128]{0,1:T(8,128)}) %all-reduce.9.cloned.1.call-update) | async-done | bytes 65552 | tf_op jit(solution)/shard_map/psum | solution.py:27
  1220.1 11.7 cholesky.81
  1233.1 9.8 custom-call.9
  1245.3 3.4 all-to-all-start.1
  1248.7 75.5 %all-reduce = (f32[1,128]{1,0:T(1,128)S(1)}, f32[1,128]{1,0:T(1,128)S(1)}, f32[1,128]{1,0:T(1,128)S(1)}) all-reduce(f32[1,128]{1,0:T(1,128)S(1)} %bitcast.216, f32[1,128]{1,0:T(1,128)S(1)} %bitcast.215, f32[1,128]{1,0:T(1,128)S(1)} %bitcast.214), channel_id=1, replica_groups=mesh['tiles'=64,'cols'=4] {'tiles','cols'}, use_global_device_ids=true, to_apply=%region_12.16 | all-reduce | flops 384 | bytes 3072 | tf_op jit(solution)/shard_map/psum | solution.py:39
  (117 shorter events, 34.9 us)
Async XLA Ops:
  11.2 10.4 all-to-all-start
  16.0 252.7 %all-reduce.5.cloned.1.call-start = ((), (), s32[]{:S(2)}) async-start(), calls=%async_computation.2 | async-start | bytes 131072 | tf_op jit(solution)/shard_map/psum | solution.py:27
  22.1 273.0 %copy-start.11 = (s32[16,8]{0,1:T(8,128)S(1)}, s32[16,8]{0,1:T(8,128)}, u32[]{:S(2)}) copy-start(s32[16,8]{0,1:T(8,128)} %param.11) | copy-start | bytes 1540
  24.2 291.6 %all-gather.7.cloned.1.call-start = ((), (), s32[]{:S(2)}) async-start(), calls=%async_computation.3 | async-start | bytes 1310720 | tf_op jit(solution)/shard_map/all_gather | solution.py:76
  295.0 192.2 %all-gather.11.cloned.1.call-start = ((), (), s32[]{:S(2)}) async-start(), calls=%async_computation.7 | async-start | bytes 16842752 | tf_op jit(solution)/shard_map/all_gather | solution.py:85
  317.5 19.5 %collective-permute-start = (bf16[128,3,256]{2,0,1:T(8,128)(2,1)S(1)}, bf16[128,3,256]{2,0,1:T(8,128)(2,1)S(1)}, u32[]{:S(2)}, u32[]{:S(2)}) collective-permute-start(bf16[128,3,256]{2,0,1:T(8,128)(2,1)S(1)} %get-tuple-element.29), channel_id=1, source_target_pairs={{0,4},{4,8},{8,12},{12,16},{16,20},{20,24},{24,28},{28,32},{32,36}... | collective-permute-start | bytes 589832 | tf_op jit(solution)/shard_map/ppermute | solution.py:17
  334.5 5.4 collective-permute-start.1
  351.9 4.3 copy-start.9
  351.9 6.0 copy-start.8
  351.9 6.0 copy-start.12
  354.0 4.5 copy-start.7
  356.2 2.9 copy-start.6
  357.9 1.7 copy-start.4
  361.6 372.0 %all-reduce.7.cloned.1.call-start = ((), (), s32[]{:S(2)}) async-start(), calls=%async_computation.4 | async-start | bytes 131072 | tf_op jit(solution)/shard_map/psum | solution.py:27
  494.9 285.8 %all-gather.9.cloned.1.call-start = ((), (), s32[]{:S(2)}) async-start(), calls=%async_computation.5 | async-start | bytes 1310720 | tf_op jit(solution)/shard_map/all_gather | solution.py:76
  759.9 206.2 %all-gather.13.cloned.1.call-start = ((), (), s32[]{:S(2)}) async-start(), calls=%async_computation.8 | async-start | bytes 33685504 | tf_op jit(solution)/shard_map/all_gather | solution.py:85
  782.4 6.6 collective-permute-start.2
  786.4 5.4 collective-permute-start.3
  803.8 4.2 copy-start.5
  803.8 6.0 copy-start.3
  803.9 6.0 copy-start.13
  805.9 4.5 copy-start.2
  808.1 2.9 copy-start.1
  809.8 1.7 copy-start
  813.7 404.6 %all-reduce.9.cloned.1.call-start = ((), (), s32[]{:S(2)}) async-start(), calls=%async_computation.6 | async-start | bytes 131072 | tf_op jit(solution)/shard_map/psum | solution.py:27
  966.1 13.6 %copy-start.10 = (f32[16,64]{1,0:T(8,128)S(1)}, f32[16,64]{1,0:T(8,128)}, u32[]{:S(2)}) copy-start(f32[16,64]{1,0:T(8,128)} %param.14) | copy-start | bytes 12292
  1245.3 79.5 %all-to-all-start.1 = ((bf16[4,2,16384]{2,1,0:T(2,128)(2,1)}), bf16[4,2,16384]{2,1,0:T(2,128)(2,1)S(1)}, u32[]{:S(2)}, u32[]{:S(2)}) async-start(bf16[4,2,16384]{2,1,0:T(2,128)(2,1)} %reshape.234), calls=%async_computation.1 | async-start | bytes 524288 | tf_op jit(solution)/shard_map/all_to_all | solution.py:100
Sparse Core Ops, SparseCore 0:
  24.4 244.3 all-reduce.4
  295.1 20.7 all-gather.6
  361.7 125.4 all-gather.10
  495.1 238.5 all-reduce.6
  760.0 20.7 all-gather.8
  813.8 152.2 all-gather.12
  979.9 238.3 all-reduce.8
